TPU v7x, 128 devices: a whole 4x4x4 slice. The times are simulated.
128 devices in a mesh: req: 16 (over y, z), mp: 8 (over x, core).
Axes of the slice: x: 4, y: 4, z: 4, core: 2. Of those that a mesh axis runs over, the one named last changes fastest.
Arguments:
- hidden_in: bfloat16 [16384, 2048], P('req', 'mp'), may hold values from -6 to 6
- w_qkv: bfloat16 [3, 2048, 2048], P(None, 'req', 'mp'), may hold values from -0.125 to 0.125
- w_out: bfloat16 [2048, 2048], P('mp', 'req'), may hold values from -0.125 to 0.125
- attn_gain: bfloat16 [2048], replicated, may hold values from 0.099609375 to 1.8984375
- mlp_gain: bfloat16 [2048], replicated, may hold values from 0.099609375 to 1.8984375
- w_gate: bfloat16 [2048, 8192], P('req', 'mp'), may hold values from -0.125 to 0.125
- w_up: bfloat16 [2048, 8192], P('req', 'mp'), may hold values from -0.125 to 0.125
- w_down: bfloat16 [8192, 2048], P('mp', 'req'), may hold values from -0.0625 to 0.0625
- k_cache: bfloat16 [16, 4096, 2048], P('req', None, 'mp'), may hold values from -363 to 363
- v_cache: bfloat16 [16, 4096, 2048], P('req', None, 'mp'), may hold values from -6 to 6
- cache_len: int32 [16], P('req'), may hold values from 256 to 4096, as said below
Outputs:
- hidden_out: bfloat16 [16384, 2048], P('req', 'mp')
- new_keys: bfloat16 [16384, 2048], P('req', 'mp')
- new_values: bfloat16 [16384, 2048], P('req', 'mp')
Inputs may be any that keep to these rules, and one draw needn't show every extreme that they name: Each request uses its first cache_len slots; later slots hold unused data. Some request's cache is full in every draw.
All inputs are finite; a program needn't handle non-finite values.
Results may differ from a plain program's by a relative error of at most 0.02.
Values may be sent and summed in bfloat16 or wider, within the bound.
No kernel may reach another device: no remote copies, remote signals or barrier semaphores. Data moves between devices by JAX's collectives and lax.ppermute only.
A program may use at most 128 MiB of HBM per device.

v0:
```python
import jax
import jax.numpy as jnp
from jax import lax
from jax.sharding import PartitionSpec as P

HD = 64
THETA = 130000.0
EPSILON = 1e-05
NEG_FILL = -1e30


def rms_scale(rows, gain):
    values = rows.astype(jnp.float32)
    meansq = jnp.mean(values * values, axis=-1, keepdims=True)
    return (values * lax.rsqrt(meansq + EPSILON) * gain.astype(jnp.float32)).astype(jnp.bfloat16)


def rotate(tensor, positions):
    half = tensor.shape[-1] // 2
    freq = THETA ** (-(jnp.arange(half, dtype=jnp.float32) * 2.0 / tensor.shape[-1]))
    angle = positions[:, None, None] * freq[None, None, :]
    cosine = jnp.cos(angle)
    sine = jnp.sin(angle)
    first = tensor[..., :half]
    second = tensor[..., half:]
    return jnp.concatenate(
        [first * cosine - second * sine, second * cosine + first * sine], axis=-1
    )


def gather_packed(blocks, axes, axis_name):
    count = lax.axis_size(axis_name)
    lane = 128
    joined = jnp.concatenate([block.reshape(-1, lane) for block in blocks], axis=0)
    gathered = lax.all_gather(joined, axis_name, axis=0, tiled=False)
    outs = []
    offset = 0
    for block, axis in zip(blocks, axes):
        rows = block.size // lane
        piece = gathered[:, offset : offset + rows].reshape((count,) + block.shape)
        piece = jnp.moveaxis(piece, 0, axis)
        shape = list(block.shape)
        shape[axis] *= count
        outs.append(piece.reshape(shape))
        offset += rows
    return outs


def absorb(carry, queries, keys, values, valid):
    top, total, accum = carry
    scores = jnp.einsum("qhd,khd->hqk", queries, keys, preferred_element_type=jnp.float32) * HD ** (
        -0.5
    )
    scores = jnp.where(valid[None], scores, NEG_FILL)
    new_top = jnp.maximum(top, jnp.max(scores, axis=-1, keepdims=True))
    factor = jnp.exp(top - new_top)
    probs = jnp.where(valid[None], jnp.exp(scores - new_top), 0.0)
    total = total * factor + jnp.sum(probs, axis=-1, keepdims=True)
    accum = accum * factor + jnp.einsum(
        "hqk,khd->hqd", probs.astype(jnp.bfloat16), values, preferred_element_type=jnp.float32
    )
    return (new_top, total, accum)


def on_device(
    hidden_in, w_qkv, w_out, attn_gain, mlp_gain, w_gate, w_up, w_down, k_cache, v_cache, cache_len
):
    new_count = hidden_in.shape[0]
    w_qkv_full = lax.all_gather(w_qkv, "req", axis=1, tiled=True)
    w_gate_full, w_up_full, w_down_full, w_out_full = gather_packed(
        [w_gate, w_up, w_down, w_out], [0, 0, 1, 1], "req"
    )
    width = w_qkv.shape[2]
    heads_local = width // HD
    slots = k_cache.shape[1]
    full_rows = lax.all_gather(hidden_in, "mp", axis=1, tiled=True)
    normed = rms_scale(full_rows, attn_gain)
    columns = normed
    projected = jnp.einsum("nd,kdw->knw", columns, w_qkv_full, preferred_element_type=jnp.float32)
    length = cache_len[0]
    positions = (length + jnp.arange(new_count, dtype=jnp.int32)).astype(jnp.float32)
    queries = rotate(projected[0].reshape(new_count, heads_local, HD), positions).astype(
        jnp.bfloat16
    )
    fresh_keys = rotate(projected[1].reshape(new_count, heads_local, HD), positions).astype(
        jnp.bfloat16
    )
    fresh_values = projected[2].astype(jnp.bfloat16).reshape(new_count, heads_local, HD)
    rows = jnp.arange(new_count, dtype=jnp.int32)
    causal = rows[:, None] >= rows[None, :]
    start_carry = (
        jnp.full((heads_local, new_count, 1), NEG_FILL, jnp.float32),
        jnp.zeros((heads_local, new_count, 1), jnp.float32),
        jnp.zeros((heads_local, new_count, HD), jnp.float32),
    )
    carry = absorb(start_carry, queries, fresh_keys, fresh_values, causal)
    cache_keys = k_cache[0].reshape(slots, heads_local, HD)
    cache_values = v_cache[0].reshape(slots, heads_local, HD)
    block = min(slots, 512)
    count = (length + block - 1) // block

    def step_block(index, state):
        begin = index * block
        keys = lax.dynamic_slice_in_dim(cache_keys, begin, block, 0)
        values = lax.dynamic_slice_in_dim(cache_values, begin, block, 0)
        valid = (begin + jnp.arange(block, dtype=jnp.int32) < length)[None, :]
        return absorb(state, queries, keys, values, valid)

    top, total, accum = lax.fori_loop(0, count, step_block, carry)
    attn = (accum / total).transpose(1, 0, 2).reshape(new_count, width).astype(jnp.bfloat16)
    partial_value = jnp.dot(attn, w_out_full, preferred_element_type=jnp.float32)
    summed = lax.psum(partial_value.astype(jnp.bfloat16), "mp").astype(jnp.float32)
    mid_full = (full_rows.astype(jnp.float32) + summed).astype(jnp.bfloat16)
    own = hidden_in.shape[1]
    mid_local = lax.dynamic_slice_in_dim(mid_full, lax.axis_index("mp") * own, own, axis=1)
    normed2 = rms_scale(mid_full, mlp_gain)
    columns = normed2
    gate = jnp.dot(columns, w_gate_full, preferred_element_type=jnp.float32)
    upper = jnp.dot(columns, w_up_full, preferred_element_type=jnp.float32)
    units = (jax.nn.silu(gate) * upper).astype(jnp.bfloat16)
    terms = jnp.dot(units, w_down_full, preferred_element_type=jnp.float32)
    reduced = lax.psum_scatter(
        terms.astype(jnp.bfloat16), "mp", scatter_dimension=1, tiled=True
    ).astype(jnp.float32)
    hidden_out = (mid_local.astype(jnp.float32) + reduced).astype(jnp.bfloat16)
    return (
        hidden_out,
        fresh_keys.reshape(new_count, width),
        fresh_values.reshape(new_count, width),
    )


def solution(mesh):
    return jax.shard_map(
        on_device,
        mesh=mesh,
        in_specs=(
            P("req", "mp"),
            P(None, "req", "mp"),
            P("mp", "req"),
            P(),
            P(),
            P("req", "mp"),
            P("req", "mp"),
            P("mp", "req"),
            P("req", None, "mp"),
            P("req", None, "mp"),
            P("req"),
        ),
        out_specs=(P("req", "mp"), P("req", "mp"), P("req", "mp")),
        check_vma=False,
    )
```

profile of v0, /device:TPU:0, one launch (start us, length us, event | category | flops | bytes accessed | tf_op | source)
XLA Modules:
  0.0 353.1 jit_solution(15132475671423839923)
XLA Ops:
  7.2 0.0 copy-start.7
  7.2 0.0 all-gather.5.cloned.1.call-start
  7.2 0.7 all-gather.5.cloned.1.call-update
  7.9 0.0 all-gather.7.cloned.1.call-start
  8.0 1.7 copy.29
  9.7 0.0 all-gather.7.cloned.1.call-update
  9.7 0.0 all-gather.9.cloned.1.call-start
  9.8 1.1 reshape.167
  10.8 1.1 reshape.168
  11.9 2.0 pad_maximum_fusion
  13.9 0.0 all-gather.9.cloned.1.call-update
  13.9 0.0 all-reduce.2.cloned.1.call-start
  14.6 0.0 copy-done.7
  14.6 2.9 copy.31
  17.6 4.1 %copy.32 = bf16[1,4096,256]{1,2,0:T(8,128)(2,1)} copy(bf16[1,4096,256]{2,1,0:T(8,128)(2,1)} %param.22) | data formatting | bytes 4194304 | tf_op args[9]
  21.7 1.3 iota_compare_fusion
  23.0 0.5 multiply_cosine_fusion
  23.5 24.7 %all-gather.5.cloned.1.call-done = bf16[1024,2048]{1,0:T(8,128)(2,1)} async-done(((bf16[1024,256]{1,0:T(8,128)(2,1)}), bf16[1024,2048]{1,0:T(8,128)(2,1)}) %all-gather.5.cloned.1.call-update) | async-done | bytes 4194320 | tf_op jit(solution)/shard_map/all_gather | solution.py:76
  48.2 3.1 fusion.26
  51.3 53.4 %all-gather.7.cloned.1.call-done = bf16[3,2048,256]{1,2,0:T(8,128)(2,1)} async-done(((bf16[3,128,256]{1,2,0:T(8,128)(2,1)}), bf16[3,2048,256]{1,2,0:T(8,128)(2,1)}) %all-gather.7.cloned.1.call-update) | async-done | bytes 3145744 | tf_op jit(solution)/shard_map/all_gather | solution.py:69
  104.7 6.6 %fusion.38 = f32[3,1024,256]{1,2,0:T(8,128)S(1)} fusion(bf16[3,2048,256]{1,2,0:T(8,128)(2,1)} %all-gather.7.cloned.1.call-done, bf16[1024,2048]{1,0:T(8,128)(2,1)} %all-gather.5.cloned.1.call-done, f32[2048]{0:T(1024)S(1)} %convert_element_type.84, f32[1024]{0:T(1024)S(1)} %add_rsqrt_fusion.1), kind=kOutput, calls=%fused_computation.52 | convolution fusion | flops 3229614080 | bytes 10498048 | tf_op jit(solution)/shard_map/nd,kdw->knw/dot_general | solution.py:79
  111.3 0.0 copy-start.3
  111.3 1.0 slice.66
  112.3 0.1 fusion.57
  112.4 0.2 subtract_convert_fusion
  112.6 0.2 multiply_subtract_fusion
  112.8 0.3 copy-done.3
  113.1 0.7 copy-done.1
  113.8 3.0 fusion.20
  116.8 0.0 copy-start.6
  116.8 4.2 %fusion.22 = f32[4,1024]{1,0:T(4,128)S(1)} fusion(f32[4,1024,1024]{1,2,0:T(8,128)S(1)} %get-tuple-element.102, f32[4,1024]{1,0:T(4,128)S(1)} %get-tuple-element.98, pred[1024,1024]{0,1:T(8,128)(4,1)S(1)} %copy-done.1), kind=kLoop, calls=%fused_computation.31 | loop fusion | flops 20967424 | bytes 17858560 | tf_op jit(solution)/shard_map/reduce_sum | solution.py:58
  121.1 0.0 copy-done.6
  121.1 5.9 %fusion.41 = f32[4,1024,64]{1,2,0:T(8,128)} fusion(bf16[1024,4,64]{0,2,1:T(8,128)(2,1)S(1)} %bitcast.91, f32[4,1024,1024]{1,2,0:T(8,128)S(1)} %get-tuple-element.102, f32[4,1024]{1,0:T(4,128)S(1)} %get-tuple-element.98, pred[1024,1024]{0,1:T(8,128)(4,1)S(1)} %copy-done.1, f32[4,1024]{1,0:T(4,128)S(1)} %get-tuple-element.96), kind=kOutput, calls=%fused_computation.53 | convolution fusion | flops 558104576 | bytes 19431424 | tf_op jit(solution)/shard_map/hqk,khd->hqd/dot_general | solution.py:59
  127.0 8.0 %while.14 = (s32[]{:T(128)}, f32[4,1024,1]{1,0,2:T(4,128)S(1)}, f32[4,1024,1]{1,0,2:T(4,128)S(1)}, f32[4,1024,64]{1,2,0:T(8,128)}, s32[]{:T(128)}, /*index=5*/s3...) while((s32[]{:T(128)}, f32[4,1024,1]{1,0,2:T(4,128)S(1)}, ...), condition=%wide.region_6.7_spmd, body=%wide.region_3.6_spmd.sunk | while | flops 564671488 | bytes 36965104 | solution.py:109
  127.0 0.7 add_compare_fusion.2
  127.7 0.0 copy-start.4
  127.7 1.6 bitcast_reduce_fusion.2
  129.3 0.0 copy-done.4
  129.3 3.1 fusion.77
  132.4 0.0 copy-start.5
  132.4 2.5 fusion.76
  135.0 1.3 divide_convert_fusion
  136.3 65.2 %all-gather.9.cloned.1.call-done = bf16[53248,128]{1,0:T(8,128)(2,1)} async-done(((bf16[3328,128]{1,0:T(8,128)(2,1)}), bf16[53248,128]{1,0:T(8,128)(2,1)}) %all-gather.9.cloned.1.call-update) | async-done | bytes 13631504 | tf_op jit(solution)/shard_map/all_gather | solution.py:35
  201.5 1.3 slice_bitcast_fusion.1
  202.8 0.5 copy.33
  203.4 3.3 convolution_convert_fusion
  206.7 0.0 all-reduce.2.cloned.1.call-update
  206.7 0.3 reduce-scatter.2.cloned.1.call-start
  207.0 0.4 copy-done.8
  207.4 9.1 %fusion.56 = (bf16[16,1024,128]{2,1,0:T(8,128)(2,1)}, bf16[1024,16,128]{2,0,1:T(8,128)(2,1)}, bf16[16,1024,128]{2,1,0:T(8,128)(2,1)}) fusion(bf16[16,3328,128]{2,1,0:T(8,128)(2,1)} %bitcast.79), kind=kLoop, calls=%fused_computation.81 | loop fusion | bytes 25165824 | tf_op jit(solution)/shard_map/slice | solution.py:40
  216.5 7.4 %reshape_reshape.6 = bf16[2048,1024]{1,0:T(8,128)(2,1)} reshape(bf16[16,1024,128]{2,1,0:T(8,128)(2,1)} %get-tuple-element.89) | data formatting | bytes 8388608 | tf_op jit(solution)/shard_map/reshape;reshape | solution.py:44
  223.9 6.4 %copy.34 = bf16[1024,16,128]{0,2,1:T(8,128)(2,1)} copy(bf16[1024,16,128]{2,0,1:T(8,128)(2,1)} %get-tuple-element.88) | data formatting | bytes 8388608 | tf_op jit(solution)/shard_map/transpose | solution.py:41
  230.4 7.4 %reshape_reshape.7 = bf16[2048,1024]{1,0:T(8,128)(2,1)} reshape(bf16[16,1024,128]{2,1,0:T(8,128)(2,1)} %get-tuple-element.87) | data formatting | bytes 8388608 | tf_op jit(solution)/shard_map/reshape;reshape | solution.py:44
  237.8 41.3 %all-reduce.2.cloned.1.call-done = bf16[1024,2048]{1,0:T(8,128)(2,1)} async-done(((bf16[1024,2048]{1,0:T(8,128)(2,1)}), bf16[1024,2048]{1,0:T(8,128)(2,1)}) %all-reduce.2.cloned.1.call-update) | async-done | bytes 4194320 | tf_op jit(solution)/shard_map/psum | solution.py:112
  279.0 5.6 %fusion.23 = (f32[1024]{0:T(1024)S(1)}, bf16[1024,2048]{1,0:T(8,128)(2,1)S(1)}) fusion(bf16[1024,2048]{1,0:T(8,128)(2,1)} %all-reduce.2.cloned.1.call-done, bf16[1024,2048]{1,0:T(8,128)(2,1)} %all-gather.5.cloned.1.call-done), kind=kLoop, calls=%fused_computation.34 | loop fusion | flops 14679040 | bytes 12587008 | tf_op jit(solution)/shard_map/reduce_sum | solution.py:14
  284.7 0.0 copy-done.2
  284.7 6.3 %fusion.45 = f32[1024,1024]{1,0:T(8,128)} fusion(bf16[2048,1024]{1,0:T(8,128)(2,1)S(1)} %copy-done.2, bf16[1024,2048]{1,0:T(8,128)(2,1)S(1)} %get-tuple-element.84, f32[2048]{0:T(1024)S(1)} %convert_element_type.99, f32[1024]{0:T(1024)S(1)} %add_rsqrt_fusion), kind=kOutput, calls=%fused_computation.54 | convolution fusion | flops 4303355904 | bytes 12595200 | tf_op jit(solution)/shard_map/dot_general | solution.py:118
  291.0 15.4 %convolution_convert_fusion.1 = bf16[1024,2048]{1,0:T(8,128)(2,1)} fusion(bf16[1024,2048]{0,1:T(8,128)(2,1)} %bitcast.84, f32[1024,1024]{1,0:T(8,128)} %fusion.45, bf16[2048,1024]{1,0:T(8,128)(2,1)} %reshape_reshape.7, bf16[1024,2048]{1,0:T(8,128)(2,1)} %copy-done, f32[2048]{0:T(1024)S(1)} %convert_element_type.99, f32[1024]{0:T(1024)S(1)} %add_rsqrt_fusion), kind=kOutput, calls=%fused_computation.51 | convolution fusion | flops 8606711808 | bytes 20983808 | tf_op jit(solution)/shard_map/dot_general | solution.py:121
  306.4 0.0 reduce-scatter.2.cloned.1.call-update
  306.4 1.0 copy.35
  307.4 1.3 slice_bitcast_fusion.2
  308.7 1.0 copy.36
  309.7 34.8 %reduce-scatter.2.cloned.1.call-done = bf16[1024,256]{1,0:T(8,128)(2,1)} async-done(((bf16[1024,2048]{1,0:T(8,128)(2,1)}), bf16[1024,256]{1,0:T(8,128)(2,1)}) %reduce-scatter.2.cloned.1.call-update) | async-done | bytes 524304 | tf_op jit(solution)/shard_map/reduce_scatter | solution.py:122
  344.5 2.1 add_convert_fusion
  (19 shorter events, 0.2 us)
Async XLA Ops:
  7.2 7.4 %copy-start.7 = (bf16[2048]{0:T(1024)(128)(2,1)S(1)}, bf16[2048]{0:T(1024)(128)(2,1)}, u32[]{:S(2)}) copy-start(bf16[2048]{0:T(1024)(128)(2,1)} %param.16) | copy-start | bytes 12292
  7.2 41.0 %all-gather.5.cloned.1.call-start = ((), (), s32[]{:S(2)}) async-start(), calls=%async_computation.1 | async-start | bytes 4718592 | tf_op jit(solution)/shard_map/all_gather | solution.py:76
  7.9 96.8 %all-gather.7.cloned.1.call-start = ((), (), s32[]{:S(2)}) async-start(), calls=%async_computation.2 | async-start | bytes 3342336 | tf_op jit(solution)/shard_map/all_gather | solution.py:69
  9.7 191.8 %all-gather.9.cloned.1.call-start = ((), (), s32[]{:S(2)}) async-start(), calls=%async_computation.5 | async-start | bytes 14483456 | tf_op jit(solution)/shard_map/all_gather | solution.py:35
  13.9 265.1 %all-reduce.2.cloned.1.call-start = ((), (), s32[]{:S(2)}) async-start(), calls=%async_computation.3 | async-start | bytes 8388608 | tf_op jit(solution)/shard_map/psum | solution.py:112
  111.3 1.8 copy-start.3
  112.3 1.5 copy-start.1
  116.8 4.2 %copy-start.6 = (bf16[1,1024,256]{1,2,0:T(8,128)(2,1)S(1)}, bf16[1,1024,256]{1,2,0:T(8,128)(2,1)}, u32[]{:S(2)}) copy-start(bf16[1,1024,256]{1,2,0:T(8,128)(2,1)} %slice.66) | copy-start | bytes 1572868
  127.7 1.6 copy-start.4
  132.4 2.6 copy-start.5
  206.7 0.7 copy-start.8
  206.7 137.7 %reduce-scatter.2.cloned.1.call-start = ((), (), s32[]{:S(2)}) async-start(), calls=%async_computation.4 | async-start | bytes 4718592 | tf_op jit(solution)/shard_map/reduce_scatter | solution.py:122
  279.0 5.6 %copy-start.2 = (bf16[2048,1024]{1,0:T(8,128)(2,1)S(1)}, bf16[2048,1024]{1,0:T(8,128)(2,1)}, u32[]{:S(2)}) copy-start(bf16[2048,1024]{1,0:T(8,128)(2,1)} %reshape_reshape.6) | copy-start | bytes 12582916
  284.6 6.4 %copy-start = (bf16[1024,2048]{1,0:T(8,128)(2,1)}, bf16[1024,2048]{1,0:T(8,128)(2,1)S(1)}, u32[]{:S(2)}) copy-start(bf16[1024,2048]{1,0:T(8,128)(2,1)S(1)} %get-tuple-element.84) | copy-start | bytes 12582916
Sparse Core Ops, SparseCore 0:
  9.7 38.4 all-gather.4
  50.9 53.7 all-gather.6
  106.9 94.6 all-gather.8
  206.9 72.1 all-reduce.1
  306.5 37.9 reduce-scatter.1
where the time goes:
time: 354 us; the launch traced here: 353 us
  waiting for transfers between devices  220 us (62%)
  local copies, waits for them, and re-layouts  48.9 us (14%)
  matrix products  45.3 us (13%)
  other arithmetic  23.8 us (7%)
  between operations  14.7 us (4%)
    all_gather x1, waiting for transfers between devices, gather_packed(): gathered = lax.all_gather(joined, axis_name, axis=0, tiled=False)  65.2 us
    all_gather x1, waiting for transfers between devices, on_device(): w_qkv_full = lax.all_gather(w_qkv, 'req', axis=1, tiled=True)  53.4 us
    psum x1, waiting for transfers between devices, on_device(): lax.psum(partial_value.astype(jnp.bfloat16), 'mp').astype(jnp.float32)  41.3 us
    reduce_scatter x1, waiting for transfers between devices, on_device(): lax.psum_scatter(terms.astype(jnp.bfloat16), 'mp', scatter_dimension=1, t...  34.8 us
    all_gather x1, waiting for transfers between devices, on_device(): full_rows = lax.all_gather(hidden_in, 'mp', axis=1, tiled=True)  24.7 us
    dot_general x1, matrix products, on_device(): terms = jnp.dot(units, w_down_full, preferred_element_type=jnp.float32)  15.4 us
    another operation x2, local copies, waits for them, and re-layouts, gather_packed(): outs.append(piece.reshape(shape))  14.8 us
    unnamed x19, local copies, waits for them, and re-layouts  12.2 us
  transfers between devices with their start and end apart: 5, of which 5 were waited for; matrix products, arithmetic and copies ran while one was open for 23% of the time, Pallas kernels for 0%

commit v1 on v0

--- a/solution.py
+++ b/solution.py
@@ -66,7 +66,8 @@
     hidden_in, w_qkv, w_out, attn_gain, mlp_gain, w_gate, w_up, w_down, k_cache, v_cache, cache_len
 ):
     new_count = hidden_in.shape[0]
-    w_qkv_full = lax.all_gather(w_qkv, "req", axis=1, tiled=True)
+    copies = jnp.concatenate([w_qkv] * lax.axis_size("req"), axis=1)
+    w_qkv_full = lax.all_to_all(copies, "req", 1, 1, tiled=True)
     w_gate_full, w_up_full, w_down_full, w_out_full = gather_packed(
         [w_gate, w_up, w_down, w_out], [0, 0, 1, 1], "req"
     )

time: 354 us -> 341 us (0.963)
  waiting for transfers between devices: 220 us -> 186 us
  local copies, waits for them, and re-layouts: 48.9 us -> 61 us
  starting transfers between devices: 0.42 us -> 8.91 us
    all_gather x1 -> x0, waiting for transfers between devices: 53.4 us -> none  [on_device(): w_qkv_full = lax.all_gather(w_qkv, 'req', axis=1, tiled=True)]
    all_to_all x0 -> x1, waiting for transfers between devices: none -> 51 us  [on_device(): w_qkv_full = lax.all_to_all(copies, 'req', 1, 1, tiled=True)]
    all_gather x1, waiting for transfers between devices: 65.2 us -> 35.8 us  [gather_packed(): gathered = lax.all_gather(joined, axis_name, axis=0, tiled=False)]
    all_gather x1, waiting for transfers between devices: 24.7 us -> 3.79 us  [on_device(): full_rows = lax.all_gather(hidden_in, 'mp', axis=1, tiled=True)]
    psum x1, waiting for transfers between devices: 41.3 us -> 59.6 us  [on_device(): lax.psum(partial_value.astype(jnp.bfloat16), 'mp').astype(jnp.float32)]
    unnamed x19 -> x35, local copies, waits for them, and re-layouts: 12.2 us -> 23.7 us
    all_to_all x0 -> x1, starting transfers between devices: none -> 8.31 us  [on_device(): w_qkv_full = lax.all_to_all(copies, 'req', 1, 1, tiled=True)]
  transfers between devices with their start and end apart: 5 -> 5, of which waited for: 5 -> 5; matrix products, arithmetic and copies ran while one was open for 23% -> 28% of each run, Pallas kernels for 0% -> 0%
where the time goes in v1:
time: 341 us; the launch traced here: 340 us
  waiting for transfers between devices  186 us (55%)
  local copies, waits for them, and re-layouts  61 us (18%)
  matrix products  45.7 us (13%)
  other arithmetic  23.8 us (7%)
  between operations  14.7 us (4%)
  starting transfers between devices  8.91 us (3%)
    psum x1, waiting for transfers between devices, on_device(): lax.psum(partial_value.astype(jnp.bfloat16), 'mp').astype(jnp.float32)  59.6 us
    all_to_all x1, waiting for transfers between devices, on_device(): w_qkv_full = lax.all_to_all(copies, 'req', 1, 1, tiled=True)  51 us
    all_gather x1, waiting for transfers between devices, gather_packed(): gathered = lax.all_gather(joined, axis_name, axis=0, tiled=False)  35.8 us
    reduce_scatter x1, waiting for transfers between devices, on_device(): lax.psum_scatter(terms.astype(jnp.bfloat16), 'mp', scatter_dimension=1, t...  34.8 us
    unnamed x35, local copies, waits for them, and re-layouts  23.7 us
    dot_general x1, matrix products, on_device(): terms = jnp.dot(units, w_down_full, preferred_element_type=jnp.float32)  15.4 us
    another operation x2, local copies, waits for them, and re-layouts, gather_packed(): outs.append(piece.reshape(shape))  14.7 us
    slice x1, local copies, waits for them, and re-layouts, gather_packed(): piece = gathered[:, offset:offset + rows].reshape((count,) + block.shape)  9.01 us
  transfers between devices with their start and end apart: 5, of which 5 were waited for; matrix products, arithmetic and copies ran while one was open for 28% of the time, Pallas kernels for 0%

profile of v1, /device:TPU:0, one launch (start us, length us, event | category | flops | bytes accessed | tf_op | source)
XLA Modules:
  0.0 339.9 jit_solution(2906134873851448980)
XLA Ops:
  7.2 0.7 all-gather.4.cloned.1.call-update
  8.0 1.1 reshape.167
  9.0 1.1 reshape.168
  10.1 2.0 pad_maximum_fusion
  12.2 0.9 constant_dynamic-update-slice_fusion.15
  13.0 0.9 constant_dynamic-update-slice_fusion.14
  13.9 0.9 constant_dynamic-update-slice_fusion.13
  14.8 0.9 constant_dynamic-update-slice_fusion.12
  15.6 0.9 constant_dynamic-update-slice_fusion.11
  16.5 0.9 constant_dynamic-update-slice_fusion.10
  17.4 0.9 constant_dynamic-update-slice_fusion.9
  18.3 0.9 constant_dynamic-update-slice_fusion.8
  19.1 0.9 constant_dynamic-update-slice_fusion.7
  20.0 0.9 constant_dynamic-update-slice_fusion.6
  20.9 0.9 constant_dynamic-update-slice_fusion.5
  21.7 0.9 constant_dynamic-update-slice_fusion.4
  22.7 0.9 constant_dynamic-update-slice_fusion.3
  23.5 0.9 constant_dynamic-update-slice_fusion.2
  24.4 0.9 constant_dynamic-update-slice_fusion.1
  25.3 0.9 constant_dynamic-update-slice_fusion
  26.2 8.3 %all-to-all-start = ((bf16[3,2048,256]{2,0,1:T(4,128)(2,1)}), bf16[3,2048,256]{2,0,1:T(4,128)(2,1)}, u32[]{:S(2)}, u32[]{:S(2)}) async-start(bf16[3,2048,256]{2,0,1:T(4,128)(2,1)} %constant_dynamic-update-slice_fusion), calls=%async_computation | async-start | bytes 8388608 | tf_op jit(solution)/shard_map/all_to_all | solution.py:70
  34.5 0.2 all-reduce.2.cloned.1.call-start
  35.4 2.9 copy.101
  38.4 4.2 %copy.102 = bf16[1,4096,256]{1,2,0:T(8,128)(2,1)} copy(bf16[1,4096,256]{2,1,0:T(8,128)(2,1)} %param.22) | data formatting | bytes 4194304 | tf_op args[9]
  42.6 1.3 iota_compare_fusion
  43.9 0.5 multiply_cosine_fusion
  44.4 3.8 %all-gather.4.cloned.1.call-done = bf16[1024,2048]{1,0:T(8,128)(2,1)} async-done(((bf16[1024,256]{1,0:T(8,128)(2,1)}), bf16[1024,2048]{1,0:T(8,128)(2,1)}) %all-gather.4.cloned.1.call-update) | async-done | bytes 4194320 | tf_op jit(solution)/shard_map/all_gather | solution.py:77
  48.2 3.1 fusion.26
  51.3 51.0 %all-to-all-done = bf16[3,2048,256]{2,0,1:T(4,128)(2,1)} async-done(((bf16[3,2048,256]{2,0,1:T(4,128)(2,1)}), bf16[3,2048,256]{2,0,1:T(4,128)(2,1)}, u32[]{:S(2)}, u32[]{:S(2)}) %all-to-all-start) | async-done | bytes 3145760 | tf_op jit(solution)/shard_map/all_to_all | solution.py:70
  102.2 7.1 %fusion.39 = f32[3,1024,256]{1,2,0:T(8,128)S(1)} fusion(bf16[1024,2048]{1,0:T(8,128)(2,1)} %all-gather.4.cloned.1.call-done, f32[2048]{0:T(1024)S(1)} %convert_element_type.84, f32[1024]{0:T(1024)S(1)} %add_rsqrt_fusion.1, bf16[3,2048,256]{2,0,1:T(4,128)(2,1)} %all-to-all-done), kind=kOutput, calls=%fused_computation.53 | convolution fusion | flops 3229614080 | bytes 10498048 | tf_op jit(solution)/shard_map/nd,kdw->knw/dot_general | solution.py:80
  109.4 0.9 slice.66
  110.3 0.1 fusion.60
  110.4 0.2 subtract_convert_fusion
  110.6 0.2 multiply_subtract_fusion
  110.8 0.4 copy-done.4
  111.2 0.7 copy-done.2
  111.9 3.0 fusion.20
  114.9 4.2 %fusion.22 = f32[4,1024]{1,0:T(4,128)S(1)} fusion(f32[4,1024,1024]{1,2,0:T(8,128)S(1)} %get-tuple-element.105, f32[4,1024]{1,0:T(4,128)S(1)} %get-tuple-element.101, pred[1024,1024]{0,1:T(8,128)(4,1)S(1)} %copy-done.2), kind=kLoop, calls=%fused_computation.31 | loop fusion | flops 20967424 | bytes 17858560 | tf_op jit(solution)/shard_map/reduce_sum | solution.py:58
  119.2 6.0 %fusion.44 = f32[4,1024,64]{1,2,0:T(8,128)} fusion(bf16[1024,4,64]{0,2,1:T(8,128)(2,1)S(1)} %bitcast.90, f32[4,1024,1024]{1,2,0:T(8,128)S(1)} %get-tuple-element.105, f32[4,1024]{1,0:T(4,128)S(1)} %get-tuple-element.101, pred[1024,1024]{0,1:T(8,128)(4,1)S(1)} %copy-done.2, f32[4,1024]{1,0:T(4,128)S(1)} %get-tuple-element.99), kind=kOutput, calls=%fused_computation.54 | convolution fusion | flops 558104576 | bytes 19431424 | tf_op jit(solution)/shard_map/hqk,khd->hqd/dot_general | solution.py:59
  125.1 8.0 %while.14 = (s32[]{:T(128)}, f32[4,1024,1]{1,0,2:T(4,128)S(1)}, f32[4,1024,1]{1,0,2:T(4,128)S(1)}, f32[4,1024,64]{1,2,0:T(8,128)}, s32[]{:T(128)}, /*index=5*/s3...) while((s32[]{:T(128)}, f32[4,1024,1]{1,0,2:T(4,128)S(1)}, ...), condition=%wide.region_6.7_spmd, body=%wide.region_3.6_spmd.sunk | while | flops 564671488 | bytes 36965104 | solution.py:110
  125.1 0.7 add_compare_fusion.2
  125.8 1.6 bitcast_reduce_fusion.2
  127.4 3.1 fusion.79
  130.5 2.5 fusion.78
  133.1 1.3 divide_convert_fusion
  134.4 35.8 %all-gather.6.cloned.1.call-done = bf16[53248,128]{1,0:T(8,128)(2,1)} async-done(((bf16[3328,128]{1,0:T(8,128)(2,1)}), bf16[53248,128]{1,0:T(8,128)(2,1)}) %all-gather.6.cloned.1.call-update) | async-done | bytes 13631504 | tf_op jit(solution)/shard_map/all_gather | solution.py:35
  170.2 1.3 slice_bitcast_fusion.1
  171.5 0.5 copy.103
  172.1 3.3 convolution_convert_fusion
  175.4 0.3 reduce-scatter.2.cloned.1.call-start
  175.7 0.3 copy-done.9
  176.1 9.0 %fusion.59 = (bf16[16,1024,128]{2,1,0:T(8,128)(2,1)}, bf16[1024,16,128]{2,0,1:T(8,128)(2,1)}, bf16[16,1024,128]{2,1,0:T(8,128)(2,1)}) fusion(bf16[16,3328,128]{2,1,0:T(8,128)(2,1)} %bitcast.78), kind=kLoop, calls=%fused_computation.98 | loop fusion | bytes 25165824 | tf_op jit(solution)/shard_map/slice | solution.py:40
  185.1 7.4 %reshape_reshape.6 = bf16[2048,1024]{1,0:T(8,128)(2,1)} reshape(bf16[16,1024,128]{2,1,0:T(8,128)(2,1)} %get-tuple-element.92) | data formatting | bytes 8388608 | tf_op jit(solution)/shard_map/reshape;reshape | solution.py:44
  192.5 6.4 %copy.104 = bf16[1024,16,128]{0,2,1:T(8,128)(2,1)} copy(bf16[1024,16,128]{2,0,1:T(8,128)(2,1)} %get-tuple-element.91) | data formatting | bytes 8388608 | tf_op jit(solution)/shard_map/transpose | solution.py:41
  198.9 7.3 %reshape_reshape.7 = bf16[2048,1024]{1,0:T(8,128)(2,1)} reshape(bf16[16,1024,128]{2,1,0:T(8,128)(2,1)} %get-tuple-element.90) | data formatting | bytes 8388608 | tf_op jit(solution)/shard_map/reshape;reshape | solution.py:44
  206.2 59.6 %all-reduce.2.cloned.1.call-done = bf16[1024,2048]{1,0:T(8,128)(2,1)} async-done(((bf16[1024,2048]{1,0:T(8,128)(2,1)}), bf16[1024,2048]{1,0:T(8,128)(2,1)}) %all-reduce.2.cloned.1.call-update) | async-done | bytes 4194320 | tf_op jit(solution)/shard_map/psum | solution.py:113
  265.8 5.6 %fusion.23 = (f32[1024]{0:T(1024)S(1)}, bf16[1024,2048]{1,0:T(8,128)(2,1)S(1)}) fusion(bf16[1024,2048]{1,0:T(8,128)(2,1)} %all-reduce.2.cloned.1.call-done, bf16[1024,2048]{1,0:T(8,128)(2,1)} %all-gather.4.cloned.1.call-done), kind=kLoop, calls=%fused_computation.34 | loop fusion | flops 14679040 | bytes 12587008 | tf_op jit(solution)/shard_map/reduce_sum | solution.py:14
  271.4 6.3 %fusion.48 = f32[1024,1024]{1,0:T(8,128)} fusion(bf16[2048,1024]{1,0:T(8,128)(2,1)S(1)} %copy-done.3, bf16[1024,2048]{1,0:T(8,128)(2,1)S(1)} %get-tuple-element.87, f32[2048]{0:T(1024)S(1)} %convert_element_type.99, f32[1024]{0:T(1024)S(1)} %add_rsqrt_fusion), kind=kOutput, calls=%fused_computation.55 | convolution fusion | flops 4303355904 | bytes 12595200 | tf_op jit(solution)/shard_map/dot_general | solution.py:119
  277.7 15.4 %convolution_convert_fusion.1 = bf16[1024,2048]{1,0:T(8,128)(2,1)} fusion(bf16[1024,2048]{0,1:T(8,128)(2,1)} %bitcast.83, f32[1024,1024]{1,0:T(8,128)} %fusion.48, bf16[2048,1024]{1,0:T(8,128)(2,1)} %reshape_reshape.7, bf16[1024,2048]{1,0:T(8,128)(2,1)} %copy-done.1, f32[2048]{0:T(1024)S(1)} %convert_element_type.99, f32[1024]{0:T(1024)S(1)} %add_rsqrt_fusion), kind=kOutput, calls=%fused_computation.51 | convolution fusion | flops 8606711808 | bytes 20983808 | tf_op jit(solution)/shard_map/dot_general | solution.py:122
  293.2 1.0 copy.105
  294.2 1.3 slice_bitcast_fusion.2
  295.5 1.0 copy.106
  296.5 34.8 %reduce-scatter.2.cloned.1.call-done = bf16[1024,256]{1,0:T(8,128)(2,1)} async-done(((bf16[1024,2048]{1,0:T(8,128)(2,1)}), bf16[1024,256]{1,0:T(8,128)(2,1)}) %reduce-scatter.2.cloned.1.call-update) | async-done | bytes 524304 | tf_op jit(solution)/shard_map/reduce_scatter | solution.py:123
  331.2 2.1 add_convert_fusion
  (35 shorter events, 0.3 us)
Async XLA Ops:
  7.2 5.0 %copy-start = (bf16[3,128,256]{2,1,0:T(8,128)(2,1)S(1)}, bf16[3,128,256]{2,1,0:T(8,128)(2,1)}, u32[]{:S(2)}) copy-start(bf16[3,128,256]{2,1,0:T(8,128)(2,1)} %param.14) | copy-start | bytes 589828
  7.2 41.0 %all-gather.4.cloned.1.call-start = ((), (), s32[]{:S(2)}) async-start(), calls=%async_computation.2 | async-start | bytes 4718592 | tf_op jit(solution)/shard_map/all_gather | solution.py:77
  7.9 162.3 %all-gather.6.cloned.1.call-start = ((), (), s32[]{:S(2)}) async-start(), calls=%async_computation.5 | async-start | bytes 14483456 | tf_op jit(solution)/shard_map/all_gather | solution.py:35
  26.2 9.2 %copy-start.8 = (bf16[2048]{0:T(1024)(128)(2,1)S(1)}, bf16[2048]{0:T(1024)(128)(2,1)}, u32[]{:S(2)}) copy-start(bf16[2048]{0:T(1024)(128)(2,1)} %param.16) | copy-start | bytes 12292
  26.2 76.0 %all-to-all-start = ((bf16[3,2048,256]{2,0,1:T(4,128)(2,1)}), bf16[3,2048,256]{2,0,1:T(4,128)(2,1)}, u32[]{:S(2)}, u32[]{:S(2)}) async-start(bf16[3,2048,256]{2,0,1:T(4,128)(2,1)} %constant_dynamic-update-slice_fusion), calls=%async_computation | async-start | bytes 8388608 | tf_op jit(solution)/shard_map/all_to_all | solution.py:70
  34.5 231.3 %all-reduce.2.cloned.1.call-start = ((), (), s32[]{:S(2)}) async-start(), calls=%async_computation.3 | async-start | bytes 8388608 | tf_op jit(solution)/shard_map/psum | solution.py:113
  109.4 1.8 copy-start.4
  110.3 1.6 copy-start.2
  114.9 4.2 %copy-start.7 = (bf16[1,1024,256]{1,2,0:T(8,128)(2,1)S(1)}, bf16[1,1024,256]{1,2,0:T(8,128)(2,1)}, u32[]{:S(2)}) copy-start(bf16[1,1024,256]{1,2,0:T(8,128)(2,1)} %slice.66) | copy-start | bytes 1572868
  125.8 1.6 copy-start.5
  130.5 2.6 copy-start.6
  175.4 0.7 copy-start.9
  175.4 155.8 %reduce-scatter.2.cloned.1.call-start = ((), (), s32[]{:S(2)}) async-start(), calls=%async_computation.4 | async-start | bytes 4718592 | tf_op jit(solution)/shard_map/reduce_scatter | solution.py:123
  265.8 5.6 %copy-start.3 = (bf16[2048,1024]{1,0:T(8,128)(2,1)S(1)}, bf16[2048,1024]{1,0:T(8,128)(2,1)}, u32[]{:S(2)}) copy-start(bf16[2048,1024]{1,0:T(8,128)(2,1)} %reshape_reshape.6) | copy-start | bytes 12582916
  271.4 6.4 %copy-start.1 = (bf16[1024,2048]{1,0:T(8,128)(2,1)}, bf16[1024,2048]{1,0:T(8,128)(2,1)S(1)}, u32[]{:S(2)}) copy-start(bf16[1024,2048]{1,0:T(8,128)(2,1)S(1)} %get-tuple-element.87) | copy-start | bytes 12582916
Sparse Core Ops, SparseCore 0:
  9.7 38.4 all-gather.3
  50.4 119.7 all-gather.5
  175.6 90.1 all-reduce.1
  293.3 37.9 reduce-scatter.1
